TPU v7x, 128 devices: a whole 4x4x4 slice. The times are simulated.
128 devices in a mesh: expert: 4 (over z_lo, core), fsdp: 32 (over y, z_hi, x).
Axes of the slice: x: 4, y: 4, z: 4 (z_hi: 2, z_lo: 2; z = z_hi * 2 + z_lo), core: 2. Of those that a mesh axis runs over, the one named last changes fastest.
Arguments:
- tokens: bfloat16 [16384, 2048], P(('expert', 'fsdp')), may hold values from -6 to 6
- expert_ids: int32 [16384, 1], P(('expert', 'fsdp')), may hold values from 0 to 7; in each aligned block of 128 rows (0 to 127, 128 to 255, ...) at most 24 rows name the same one
- gate_weight: bfloat16 [8, 2048, 8192], P('expert', None, 'fsdp'), may hold values from -0.125 to 0.125
- up_weight: bfloat16 [8, 2048, 8192], P('expert', None, 'fsdp'), may hold values from -0.125 to 0.125
- hidden_grad: bfloat16 [8, 3072, 8192], P('expert', None, 'fsdp'), may hold values from -0.1796875 to 0.1796875
Outputs:
- hidden: bfloat16 [8, 3072, 8192], P('expert', None, 'fsdp')
- gate_grad: float32 [8, 2048, 8192], P('expert', None, 'fsdp')
- up_grad: float32 [8, 2048, 8192], P('expert', None, 'fsdp')
Inputs may be any that keep to these rules, and one draw needn't show every extreme that they name: `expert_ids`: within the tokens of one device (aligned blocks of 128 rows) no expert is named more than 24 times, a bound that some block reaches.
All inputs are finite; a program needn't handle non-finite values.
Results may differ from a plain program's by a relative error of at most 0.003.
Values may be sent and summed in bfloat16 or wider, within the bound.
No kernel may reach another device: no remote copies, remote signals or barrier semaphores. Data moves between devices by JAX's collectives and lax.ppermute only.
A program may use at most 192 MiB of HBM per device.

v0:
```python
import jax
import jax.numpy as jnp
from jax import lax
from jax.sharding import PartitionSpec as P

CAP = 24


def make_fold(gate_part, up_part, grad_part, piece):
    groups, sources, count, model = piece.shape
    rows_flat = piece.reshape(groups, sources * count, model)
    gate = jnp.einsum("grd,gdf->grf", rows_flat, gate_part, preferred_element_type=jnp.float32)
    upval = jnp.einsum("grd,gdf->grf", rows_flat, up_part, preferred_element_type=jnp.float32)
    cotan = grad_part
    cotan = cotan.reshape(groups, sources * count, cotan.shape[3]).astype(jnp.float32)
    sigma = 1.0 / (1.0 + jnp.exp(-gate))
    active = gate * sigma
    hidden = (active * upval).astype(jnp.bfloat16)
    gate_delta = (cotan * upval * sigma * (1.0 + gate * (1.0 - sigma))).astype(jnp.bfloat16)
    up_delta = (cotan * active).astype(jnp.bfloat16)
    hidden_buf = hidden.reshape(groups, sources, count, hidden.shape[2])
    gate_sum = jnp.einsum("grd,grf->gdf", rows_flat, gate_delta, preferred_element_type=jnp.float32)
    up_sum = jnp.einsum("grd,grf->gdf", rows_flat, up_delta, preferred_element_type=jnp.float32)
    return (hidden_buf, gate_sum, up_sum)


def on_device(tokens, expert_ids, gate_weight, up_weight, hidden_grad):
    owners = lax.axis_size("expert")
    members = lax.axis_size("fsdp")
    per_owner = gate_weight.shape[0]
    model = gate_weight.shape[1]
    width = gate_weight.shape[2]
    route = expert_ids[:, 0]
    total_experts = per_owner * owners
    onehot = (route[:, None] == jnp.arange(total_experts, dtype=jnp.int32)[None, :]).astype(
        jnp.int32
    )
    rank = jnp.sum((jnp.cumsum(onehot, axis=0) - onehot) * onehot, axis=1)
    owner_of = route // per_owner
    within = route % per_owner
    target = within * (owners * CAP) + owner_of * CAP + rank
    send_rows = per_owner * owners * CAP
    placing = (jnp.arange(send_rows, dtype=jnp.int32)[:, None] == target[None, :]).astype(
        jnp.bfloat16
    )
    outgoing = jnp.dot(placing, tokens, preferred_element_type=jnp.float32).astype(jnp.bfloat16)
    outgoing = outgoing.reshape(per_owner, owners, CAP, model)
    slot_count = members * CAP
    grad_four = hidden_grad.reshape(per_owner, owners, slot_count, width)
    arrived = lax.all_to_all(outgoing, "expert", split_axis=1, concat_axis=1, tiled=True)
    hidden_buf, gate_sum, up_sum = make_fold(
        gate_weight, up_weight, grad_four, lax.all_gather(arrived, "fsdp", axis=2, tiled=True)
    )
    hidden = hidden_buf.reshape(per_owner, owners * slot_count, width)
    return (hidden, gate_sum, up_sum)


def solution(mesh):
    in_specs = (
        P(("expert", "fsdp"), None),
        P(("expert", "fsdp"), None),
        P("expert", None, "fsdp"),
        P("expert", None, "fsdp"),
        P("expert", None, "fsdp"),
    )
    out_specs = (P("expert", None, "fsdp"), P("expert", None, "fsdp"), P("expert", None, "fsdp"))
    return jax.shard_map(
        on_device, mesh=mesh, in_specs=in_specs, out_specs=out_specs, check_vma=False
    )
```

profile of v0, /device:TPU:1, one launch (start us, length us, event | category | flops | bytes accessed | tf_op | source)
XLA Modules:
  0.0 333.2 jit_solution(6977620930434274134)
XLA Ops:
  7.2 0.0 copy-start
  7.2 0.0 all-gather.2.cloned.1.call-start
  7.2 0.9 fusion.11
  8.1 0.2 reduce_window_sum.11
  8.3 0.8 select_reduce_fusion
  9.1 0.7 fusion.15
  9.8 1.4 convolution_convert_fusion
  11.2 0.1 copy.10
  11.3 15.2 %all_to_all.5 = bf16[2,4,24,2048]{3,2,0,1:T(8,128)(2,1)} all-to-all(bf16[2,4,24,2048]{3,2,0,1:T(8,128)(2,1)S(1)} %copy.10), channel_id=1, replica_groups=mesh['expert'=4,'fsdp'=32] {'expert'}, dimensions={1} | all-to-all | bytes 1572864 | tf_op jit(solution)/shard_map/all_to_all | solution.py:50
  26.5 0.0 all-gather.2.cloned.1.call-update
  26.5 211.1 %all-gather.2.cloned.1.call-done = bf16[2,4,768,2048]{3,2,0,1:T(8,128)(2,1)} async-done(((bf16[2,4,24,2048]{3,2,0,1:T(8,128)(2,1)}), bf16[2,4,768,2048]{3,2,0,1:T(8,128)(2,1)}) %all-gather.2.cloned.1.call-update) | async-done | bytes 25165840 | tf_op jit(solution)/shard_map/all_gather | solution.py:52
  237.6 0.0 copy-start.3
  237.6 21.2 %copy.11 = bf16[2,4,768,2048]{3,2,1,0:T(8,128)(2,1)} copy(bf16[2,4,768,2048]{3,2,0,1:T(8,128)(2,1)} %all-gather.2.cloned.1.call-done) | data formatting | bytes 50331648 | tf_op jit(solution)/shard_map/all_gather | solution.py:52
  258.8 0.0 copy-done.3
  258.8 0.0 copy-start.2
  258.8 14.5 %fusion.18 = f32[2,3072,256]{2,1,0:T(8,128)} fusion(bf16[2,3072,2048]{2,1,0:T(8,128)(2,1)} %bitcast.11, bf16[2,2048,256]{2,1,0:T(8,128)(2,1)S(1)} %copy-done.3), kind=kOutput, calls=%fused_computation.28 | convolution fusion | flops 6442450944 | bytes 33554432 | tf_op jit(solution)/shard_map/grd,gdf->grf/dot_general | solution.py:12
  273.3 0.0 copy-done.2
  273.3 17.5 %fusion.5 = f32[2,2048,256]{2,1,0:T(8,128)} fusion(bf16[2,3072,2048]{2,1,0:T(8,128)(2,1)} %bitcast.12, bf16[2,3072,256]{2,1,0:T(8,128)(2,1)S(1)} %copy-done.2, f32[2,3072,256]{2,1,0:T(8,128)} %fusion.18), kind=kOutput, calls=%fused_computation.9 | convolution fusion | flops 6453460992 | bytes 38797312 | tf_op jit(solution)/shard_map/grd,grf->gdf/dot_general | solution.py:23
  290.8 0.0 copy-done
  290.8 16.1 %multiply_convert_fusion = (bf16[2,3072,256]{2,1,0:T(8,128)(2,1)}, f32[2,3072,256]{2,1,0:T(8,128)}) fusion(f32[2,3072,256]{2,1,0:T(8,128)} %fusion.18, bf16[2,3072,2048]{2,1,0:T(8,128)(2,1)} %bitcast.13, bf16[2,2048,256]{2,1,0:T(8,128)(2,1)S(1)} %copy-done), kind=kOutput, calls=%fused_computation.6 | convolution fusion | flops 6451888128 | bytes 42991616 | tf_op jit(solution)/shard_map/grd,gdf->grf/dot_general | solution.py:13
  306.8 0.0 copy-start.1
  306.8 19.5 %fusion.7 = f32[2,2048,256]{2,1,0:T(8,128)} fusion(bf16[2,3072,2048]{2,1,0:T(8,128)(2,1)} %bitcast.14, f32[2,3072,256]{2,1,0:T(8,128)} %get-tuple-element.4, bf16[2,3072,256]{2,1,0:T(8,128)(2,1)S(1)} %copy-done.2, f32[2,3072,256]{2,1,0:T(8,128)} %fusion.18), kind=kOutput, calls=%fused_computation.10 | convolution fusion | flops 6459752448 | bytes 45088768 | tf_op jit(solution)/shard_map/grd,grf->gdf/dot_general | solution.py:22
  326.4 0.0 copy-done.1
Async XLA Ops:
  7.2 283.6 %copy-start = (bf16[2,2048,256]{2,1,0:T(8,128)(2,1)S(1)}, bf16[2,2048,256]{2,1,0:T(8,128)(2,1)}, u32[]{:S(2)}) copy-start(bf16[2,2048,256]{2,1,0:T(8,128)(2,1)} %param.8) | copy-start | bytes 6291460
  7.2 230.5 %all-gather.2.cloned.1.call-start = ((), (), s32[]{:S(2)}) async-start(), calls=%async_computation.1 | async-start | bytes 25952256 | tf_op jit(solution)/shard_map/all_gather | solution.py:52
  237.6 21.2 %copy-start.3 = (bf16[2,2048,256]{2,1,0:T(8,128)(2,1)S(1)}, bf16[2,2048,256]{2,1,0:T(8,128)(2,1)}, u32[]{:S(2)}) copy-start(bf16[2,2048,256]{2,1,0:T(8,128)(2,1)} %param.7) | copy-start | bytes 6291460
  258.8 14.5 %copy-start.2 = (bf16[2,3072,256]{2,1,0:T(8,128)(2,1)S(1)}, bf16[2,3072,256]{2,1,0:T(8,128)(2,1)}, u32[]{:S(2)}) copy-start(bf16[2,3072,256]{2,1,0:T(8,128)(2,1)} %param.9) | copy-start | bytes 9437188
  306.8 19.5 %copy-start.1 = (bf16[2,2048,256]{2,1,0:T(8,128)(2,1)S(1)}, bf16[2,2048,256]{2,1,0:T(8,128)(2,1)}, u32[]{:S(2)}) copy-start(bf16[2,2048,256]{2,1,0:T(8,128)(2,1)} %param.8) | copy-start | bytes 6291460
Sparse Core Ops, SparseCore 0:
  26.6 210.9 all-gather.1
where the time goes:
time: 334 us; the launch traced here: 333 us
  waiting for transfers between devices  211 us (63%)
  matrix products  68.9 us (21%)
  local copies, waits for them, and re-layouts  21.3 us (6%)
  blocking collectives  15.2 us (5%)
  between operations  14.1 us (4%)
    all_gather x1, waiting for transfers between devices, on_device(): lax.all_gather(arrived, 'fsdp', axis=2, tiled=True)  211 us
    all_gather x1, local copies, waits for them, and re-layouts, on_device(): lax.all_gather(arrived, 'fsdp', axis=2, tiled=True)  21.2 us
    dot_general x1, matrix products, make_fold(): jnp.einsum('grd,grf->gdf', rows_flat, gate_delta, preferred_element_type=...  19.5 us
    dot_general x1, matrix products, make_fold(): jnp.einsum('grd,grf->gdf', rows_flat, up_delta, preferred_element_type=jn...  17.5 us
    dot_general x1, matrix products, make_fold(): jnp.einsum('grd,gdf->grf', rows_flat, up_part, preferred_element_type=jnp...  16.1 us
    all_to_all x1, blocking collectives, on_device(): lax.all_to_all(outgoing, 'expert', split_axis=1, concat_axis=1, tiled=True)  15.2 us
    dot_general x1, matrix products, make_fold(): jnp.einsum('grd,gdf->grf', rows_flat, gate_part, preferred_element_type=j...  14.5 us
  transfers between devices with their start and end apart: 1, of which 1 were waited for; matrix products, arithmetic and copies ran while one was open for 0% of the time, Pallas kernels for 0%

commit v1 on v0

--- a/solution.py
+++ b/solution.py
@@ -4,6 +4,12 @@
 from jax.sharding import PartitionSpec as P
 
 CAP = 24
+
+
+def marks_use(dim_i, tile_in):
+    part_next = jnp.stack([tile_in for _ in range(jax.lax.axis_size("fsdp"))])
+    b_next = jax.lax.all_to_all(part_next, "fsdp", 0, 0)
+    return jnp.concatenate(b_next, axis=dim_i)
 
 
 def make_fold(gate_part, up_part, grad_part, piece):
@@ -49,7 +55,7 @@
     grad_four = hidden_grad.reshape(per_owner, owners, slot_count, width)
     arrived = lax.all_to_all(outgoing, "expert", split_axis=1, concat_axis=1, tiled=True)
     hidden_buf, gate_sum, up_sum = make_fold(
-        gate_weight, up_weight, grad_four, lax.all_gather(arrived, "fsdp", axis=2, tiled=True)
+        gate_weight, up_weight, grad_four, marks_use(2, arrived)
     )
     hidden = hidden_buf.reshape(per_owner, owners * slot_count, width)
     return (hidden, gate_sum, up_sum)

time: 334 us -> 408 us (1.22)
  the two profiles are of different devices: /device:TPU:1 before, /device:TPU:34 now
where the time goes in v1:
time: 408 us; the launch traced here: 407 us
  blocking collectives  311 us (76%)
  matrix products  68.7 us (17%)
  local copies, waits for them, and re-layouts  24.5 us (6%)
    all_to_all x1, blocking collectives, marks_use(): b_next = jax.lax.all_to_all(part_next, 'fsdp', 0, 0)  298 us
    reshape x1, local copies, waits for them, and re-layouts, marks_use(): return jnp.concatenate(b_next, axis=dim_i)  21.2 us
    dot_general x1, matrix products, make_fold(): jnp.einsum('grd,grf->gdf', rows_flat, gate_delta, preferred_element_type=...  19.2 us
    dot_general x1, matrix products, make_fold(): jnp.einsum('grd,grf->gdf', rows_flat, up_delta, preferred_element_type=jn...  17.5 us
    dot_general x1, matrix products, make_fold(): jnp.einsum('grd,gdf->grf', rows_flat, up_part, preferred_element_type=jnp...  16.1 us
    dot_general x1, matrix products, make_fold(): jnp.einsum('grd,gdf->grf', rows_flat, gate_part, preferred_element_type=j...  14.5 us
    all_to_all x1, blocking collectives, on_device(): lax.all_to_all(outgoing, 'expert', split_axis=1, concat_axis=1, tiled=True)  13.1 us

profile of v1, /device:TPU:34, one launch (start us, length us, event | category | flops | bytes accessed | tf_op | source)
XLA Modules:
  0.0 407.3 jit_solution(7129477333178125525)
XLA Ops:
  0.6 0.0 copy-start
  0.6 0.9 fusion.11
  1.5 0.2 reduce_window_sum.11
  1.7 0.8 select_reduce_fusion
  2.5 0.7 fusion.15
  3.2 1.4 convolution_convert_fusion
  4.6 0.1 copy.10
  4.7 13.1 %all_to_all.10 = bf16[2,4,24,2048]{3,2,0,1:T(8,128)(2,1)S(1)} all-to-all(bf16[2,4,24,2048]{3,2,0,1:T(8,128)(2,1)S(1)} %copy.10), channel_id=1, replica_groups=mesh['expert'=4,'fsdp'=32] {'expert'}, dimensions={1} | all-to-all | bytes 1572864 | tf_op jit(solution)/shard_map/all_to_all | solution.py:56
  17.8 0.1 copy.11
  17.8 3.2 stack.2
  21.0 297.8 %all_to_all.11 = bf16[32,2,4,24,2048]{4,3,2,1,0:T(8,128)(2,1)} all-to-all(bf16[32,2,4,24,2048]{4,3,2,1,0:T(8,128)(2,1)S(1)} %stack.2), channel_id=1, replica_groups=mesh['expert'=4,'fsdp'=32] {'fsdp'}, dimensions={0} | all-to-all | bytes 50331648 | tf_op jit(solution)/shard_map/all_to_all | solution.py:11
  318.8 0.0 copy-start.2
  318.8 21.2 %copy.12 = bf16[2,4,32,24,2048]{4,3,2,1,0:T(8,128)(2,1)} copy(bf16[2,4,32,24,2048]{4,3,1,0,2:T(8,128)(2,1)} %bitcast.12) | data formatting | bytes 50331648 | tf_op jit(solution)/shard_map/reshape | solution.py:12
  340.0 0.0 copy-done.2
  340.0 0.0 copy-start.1
  340.1 14.5 %fusion.18 = f32[2,3072,256]{2,1,0:T(8,128)} fusion(bf16[2,3072,2048]{2,1,0:T(8,128)(2,1)} %bitcast.13, bf16[2,2048,256]{2,1,0:T(8,128)(2,1)S(1)} %copy-done.2), kind=kOutput, calls=%fused_computation.28 | convolution fusion | flops 6442450944 | bytes 33554432 | tf_op jit(solution)/shard_map/grd,gdf->grf/dot_general | solution.py:18
  354.6 0.0 copy-done.1
  354.6 17.5 %fusion.5 = f32[2,2048,256]{2,1,0:T(8,128)} fusion(bf16[2,3072,2048]{2,1,0:T(8,128)(2,1)} %bitcast.14, bf16[2,3072,256]{2,1,0:T(8,128)(2,1)S(1)} %copy-done.1, f32[2,3072,256]{2,1,0:T(8,128)} %fusion.18), kind=kOutput, calls=%fused_computation.9 | convolution fusion | flops 6453460992 | bytes 38797312 | tf_op jit(solution)/shard_map/grd,grf->gdf/dot_general | solution.py:29
  372.0 0.0 copy-done
  372.0 16.1 %multiply_convert_fusion = (bf16[2,3072,256]{2,1,0:T(8,128)(2,1)}, f32[2,3072,256]{2,1,0:T(8,128)}) fusion(f32[2,3072,256]{2,1,0:T(8,128)} %fusion.18, bf16[2,3072,2048]{2,1,0:T(8,128)(2,1)} %bitcast.15, bf16[2,2048,256]{2,1,0:T(8,128)(2,1)S(1)} %copy-done), kind=kOutput, calls=%fused_computation.6 | convolution fusion | flops 6451888128 | bytes 42991616 | tf_op jit(solution)/shard_map/grd,gdf->grf/dot_general | solution.py:19
  388.1 19.2 %fusion.7 = f32[2,2048,256]{2,1,0:T(8,128)} fusion(bf16[2,3072,2048]{2,1,0:T(8,128)(2,1)} %bitcast.16, f32[2,3072,256]{2,1,0:T(8,128)} %get-tuple-element.4, bf16[2,3072,256]{2,1,0:T(8,128)(2,1)S(1)} %copy-done.1, f32[2,3072,256]{2,1,0:T(8,128)} %fusion.18), kind=kOutput, calls=%fused_computation.10 | convolution fusion | flops 6459752448 | bytes 45088768 | tf_op jit(solution)/shard_map/grd,grf->gdf/dot_general | solution.py:28
Async XLA Ops:
  0.6 371.4 %copy-start = (bf16[2,2048,256]{2,1,0:T(8,128)(2,1)S(1)}, bf16[2,2048,256]{2,1,0:T(8,128)(2,1)}, u32[]{:S(2)}) copy-start(bf16[2,2048,256]{2,1,0:T(8,128)(2,1)} %param.8) | copy-start | bytes 6291460
  318.8 21.2 %copy-start.2 = (bf16[2,2048,256]{2,1,0:T(8,128)(2,1)S(1)}, bf16[2,2048,256]{2,1,0:T(8,128)(2,1)}, u32[]{:S(2)}) copy-start(bf16[2,2048,256]{2,1,0:T(8,128)(2,1)} %param.7) | copy-start | bytes 6291460
  340.0 14.5 %copy-start.1 = (bf16[2,3072,256]{2,1,0:T(8,128)(2,1)S(1)}, bf16[2,3072,256]{2,1,0:T(8,128)(2,1)}, u32[]{:S(2)}) copy-start(bf16[2,3072,256]{2,1,0:T(8,128)(2,1)} %param.9) | copy-start | bytes 9437188
